TPU v7x, 256 devices: a whole 4x4x8 slice. The times are simulated.
256 devices in a mesh: seq: 64 (over x, z, core), mp: 4 (over y).
Axes of the slice: x: 4, y: 4, z: 8, core: 2. Of those that a mesh axis runs over, the one named last changes fastest.
Arguments:
- states: bfloat16 [4, 128, 2560], P(None, 'seq', 'mp'), may hold values from -6 to 6
- norm_gain: float32 [2560], replicated, may hold values from 0.5 to 2
- query_gain: float32 [128], replicated, may hold values from 0.7 to 2
- key_gain: float32 [128], replicated, may hold values from 0.7 to 2
- w_query: bfloat16 [2560, 2048], P(None, 'mp'), may hold values from -0.125 to 0.125
- key_matrix: bfloat16 [2560, 512], P(None, 'mp'), may hold values from -0.125 to 0.125
- value_matrix: bfloat16 [2560, 512], P(None, 'mp'), may hold values from -0.125 to 0.125
- w_out: bfloat16 [2048, 2560], P('mp'), may hold values from -0.125 to 0.125
- cached_key_blocks: bfloat16 [1024, 256, 512], P('seq', None, 'mp'), may hold values from -216 to 216
- cached_value_blocks: bfloat16 [1024, 256, 512], P('seq', None, 'mp'), may hold values from -6 to 6
- req_len: int32 [128], replicated, may hold values from 1 to 16384, as said below
- slot_request: int32 [1024], P('seq'), may hold values from 0 to 127, as said below
- slot_block: int32 [1024], P('seq'), may hold values from 0 to 63
- slot_empty: int32 [1024], P('seq'), may hold values from 0 to 1
Outputs:
- hidden: bfloat16 [4, 128, 2560], P(None, 'seq', 'mp')
- new_keys: bfloat16 [4, 128, 512], P(None, 'seq', 'mp')
- new_values: bfloat16 [4, 128, 512], P(None, 'seq', 'mp')
Inputs may be any that keep to these rules, and one draw needn't show every extreme that they name: `req_len`: exactly 12 requests have length 16384; each other request has length at most 511, and one of them exactly that. Slot s holds positions slot_block[s] * 256 onward of request slot_request[s] unless slot_empty[s] = 1. Each block of a request below its length lies in exactly one slot that is not empty. A request of length 16384 has one block on every index of seq; every block of any other request b lies on index b // 2 of seq.
All inputs are finite; a program needn't handle non-finite values.
Results may differ from a plain program's by a relative error of at most 0.0098.
Values may be sent and summed in bfloat16 or wider, within the bound.
No kernel may reach another device: no remote copies, remote signals or barrier semaphores. Data moves between devices by JAX's collectives and lax.ppermute only.
A program may use at most 64 MiB of HBM per device.

v0:
```python
import jax
import jax.numpy as jnp
from jax import lax
from jax.sharding import PartitionSpec as P

HEAD_SIZE = 128
STEPS = 4
ROPE_BASE = 1000000.0
NEGATIVE = -1e30
HIGHEST = lax.Precision.HIGHEST


def scaled_rms(values, gain):
    return values * lax.rsqrt(jnp.mean(values * values, axis=-1, keepdims=True) + 1e-06) * gain


def rotate(values, positions):
    halfway = values.shape[-1] // 2
    frequency = ROPE_BASE ** (-(jnp.arange(halfway, dtype=jnp.float32) * 2.0) / values.shape[-1])
    angles = positions.astype(jnp.float32)[..., None, None] * frequency
    cosine = jnp.cos(angles)
    sine_part = jnp.sin(angles)
    leading = values[..., :halfway]
    trailing = values[..., halfway:]
    return jnp.concatenate(
        [leading * cosine - trailing * sine_part, trailing * cosine + leading * sine_part], axis=-1
    )


def project(inputs, positions, norm_gain, query_gain, key_gain, w_query, key_matrix, value_matrix):
    number = inputs.shape[0]
    normed = scaled_rms(inputs.astype(jnp.float32), norm_gain).astype(jnp.bfloat16)
    query_rows = jnp.dot(normed, w_query, preferred_element_type=jnp.float32).reshape(
        number, -1, HEAD_SIZE
    )
    keys = jnp.dot(normed, key_matrix, preferred_element_type=jnp.float32).reshape(
        number, -1, HEAD_SIZE
    )
    values = jnp.dot(normed, value_matrix, preferred_element_type=jnp.float32).astype(jnp.bfloat16)
    query_rows = (
        rotate(scaled_rms(query_rows, query_gain), positions)
        .reshape(number, -1)
        .astype(jnp.bfloat16)
    )
    keys = rotate(scaled_rms(keys, key_gain), positions).reshape(number, -1).astype(jnp.bfloat16)
    return (query_rows, keys, values)


def shards(
    states,
    norm_gain,
    query_gain,
    key_gain,
    w_query,
    key_matrix,
    value_matrix,
    w_out,
    cached_key_blocks,
    cached_value_blocks,
    req_len,
    slot_request,
    slot_block,
    slot_empty,
):
    own_rows = states.shape[1]
    first_row = lax.axis_index("seq") * own_rows
    kv_heads = key_matrix.shape[1] // HEAD_SIZE
    q_heads = w_query.shape[1] // HEAD_SIZE
    head_sharing = q_heads // kv_heads
    query_width = w_query.shape[1]
    kv_width = key_matrix.shape[1]
    slot_count = cached_key_blocks.shape[0]
    block_len = cached_key_blocks.shape[1]
    requests = req_len.shape[0]
    scaling = HEAD_SIZE ** (-0.5)
    slot_len = jnp.take(req_len, slot_request)
    offsets = jnp.arange(block_len, dtype=jnp.int32)
    filled = (slot_empty[:, None] == 0) & (
        slot_block[:, None] * block_len + offsets[None, :] < slot_len[:, None]
    )
    filled_wide = filled[None, :, None, None, :]
    belongs = (slot_request[None, :] == jnp.arange(requests, dtype=jnp.int32)[:, None]) & (
        slot_empty[None, :] == 0
    )
    belongs_float = belongs.astype(jnp.float32)
    keys_split = cached_key_blocks.reshape(slot_count, block_len, kv_heads, HEAD_SIZE)
    values_split = cached_value_blocks.reshape(slot_count, block_len, kv_heads, HEAD_SIZE)
    turn_spans = [(sequence_index, sequence_index + 1) for sequence_index in range(STEPS)]
    past_keys = []
    past_values = []
    results = []
    for low_turn, high_turn in turn_spans:
        number = high_turn - low_turn
        turn_ids = jnp.arange(low_turn, high_turn, dtype=jnp.int32)
        block_states = states[low_turn:high_turn]
        wide_states = lax.all_gather(block_states, "mp", axis=2, tiled=True)
        portion = lax.all_gather(wide_states, "seq", axis=1, tiled=True)
        portion_rows = portion.shape[1]
        portion_positions = req_len[None, :] + turn_ids[:, None]
        part_query, part_key, part_value = project(
            portion.reshape(number * portion_rows, -1),
            portion_positions.reshape(-1),
            norm_gain,
            query_gain,
            key_gain,
            w_query,
            key_matrix,
            value_matrix,
        )
        everyone = jnp.concatenate([part_query, part_key, part_value], axis=1).reshape(
            number, portion_rows, -1
        )
        own_packed = lax.dynamic_slice_in_dim(everyone, first_row, own_rows, 1)
        all_query = everyone[:, :, :query_width]
        own_heads = own_packed[:, :, :query_width].reshape(
            number, own_rows, kv_heads, head_sharing, HEAD_SIZE
        )
        past_keys.append(own_packed[:, :, query_width : query_width + kv_width])
        past_values.append(own_packed[:, :, query_width + kv_width :])
        slot_query = jnp.take(all_query, slot_request, axis=1).reshape(
            number, slot_count, kv_heads, head_sharing, HEAD_SIZE
        )
        scores = (
            jnp.einsum(
                "tsngd,sknd->tsngk", slot_query, keys_split, preferred_element_type=jnp.float32
            )
            * scaling
        )
        slot_maximum = jnp.max(jnp.where(filled_wide, scores, NEGATIVE), axis=-1)
        row_top = jnp.max(
            jnp.where(belongs[None, :, :, None, None], slot_maximum[:, None], NEGATIVE), axis=2
        )
        slot_reference = jnp.take(row_top, slot_request, axis=1)
        weights = jnp.where(
            filled_wide,
            jnp.exp(jnp.where(filled_wide, scores - slot_reference[..., None], 0.0)),
            0.0,
        )
        slot_total = jnp.sum(weights, axis=-1)
        slot_mix = jnp.einsum(
            "tsngk,sknd->tsngd",
            weights.astype(jnp.bfloat16),
            values_split,
            preferred_element_type=jnp.float32,
        )
        row_total = jnp.einsum("bs,tsng->tbng", belongs_float, slot_total, precision=HIGHEST)
        row_mix = jnp.einsum("bs,tsngd->tbngd", belongs_float, slot_mix, precision=HIGHEST)
        every_top = lax.pmax(row_top, "seq")
        every_factor = jnp.exp(row_top - every_top)
        summed_total, summed_mix = lax.psum(
            (row_total * every_factor, row_mix * every_factor[..., None]), "seq"
        )
        own_top = lax.dynamic_slice_in_dim(every_top, first_row, own_rows, 1)
        own_total = lax.dynamic_slice_in_dim(summed_total, first_row, own_rows, 1)
        own_mix = lax.dynamic_slice_in_dim(summed_mix, first_row, own_rows, 1)
        earlier_keys = jnp.concatenate(past_keys, axis=0).reshape(
            high_turn, own_rows, kv_heads, HEAD_SIZE
        )
        earlier_values = jnp.concatenate(past_values, axis=0).reshape(
            high_turn, own_rows, kv_heads, HEAD_SIZE
        )
        fresh_scores = (
            jnp.einsum(
                "trngd,jrnd->trngj", own_heads, earlier_keys, preferred_element_type=jnp.float32
            )
            * scaling
        )
        allowed = (jnp.arange(high_turn, dtype=jnp.int32)[None, :] <= turn_ids[:, None])[
            :, None, None, None, :
        ]
        fresh_top = jnp.max(jnp.where(allowed, fresh_scores, NEGATIVE), axis=-1)
        overall = jnp.maximum(own_top, fresh_top)
        retained = jnp.exp(own_top - overall)
        fresh_weights = jnp.where(
            allowed, jnp.exp(jnp.where(allowed, fresh_scores - overall[..., None], 0.0)), 0.0
        )
        denominator = own_total * retained + jnp.sum(fresh_weights, axis=-1)
        mixture = own_mix * retained[..., None] + jnp.einsum(
            "trngj,jrnd->trngd",
            fresh_weights.astype(jnp.bfloat16),
            earlier_values,
            preferred_element_type=jnp.float32,
        )
        attended = (
            (mixture / denominator[..., None])
            .astype(jnp.bfloat16)
            .reshape(number * own_rows, query_width)
        )
        projected_out = jnp.dot(attended, w_out, preferred_element_type=jnp.float32).reshape(
            number, own_rows, -1
        )
        summed = lax.psum_scatter(projected_out, "mp", scatter_dimension=2, tiled=True)
        results.append((block_states.astype(jnp.float32) + summed).astype(jnp.bfloat16))
    return (
        jnp.concatenate(results, axis=0),
        jnp.concatenate(past_keys, axis=0),
        jnp.concatenate(past_values, axis=0),
    )


def solution(mesh):
    placed = (
        P(None, "seq", "mp"),
        P(),
        P(),
        P(),
        P(None, "mp"),
        P(None, "mp"),
        P(None, "mp"),
        P("mp", None),
        P("seq", None, "mp"),
        P("seq", None, "mp"),
        P(),
        P("seq"),
        P("seq"),
        P("seq"),
    )
    return jax.shard_map(
        shards,
        mesh=mesh,
        in_specs=placed,
        out_specs=(P(None, "seq", "mp"), P(None, "seq", "mp"), P(None, "seq", "mp")),
        check_vma=False,
    )
```

profile of v0, /device:TPU:2, one launch (start us, length us, event | category | flops | bytes accessed | tf_op | source)
XLA Modules:
  0.0 764.8 jit_solution(867895954115995821)
XLA Ops:
  8.8 12.3 %all_gather.28 = bf16[1,2,2560]{2,0,1:T(2,128)(2,1)S(1)} all-gather(bf16[1,2,640]{2,0,1:T(2,128)(2,1)S(1)} %copy.475), channel_id=1, replica_groups=mesh['seq'=64,'mp'=4] {'mp'}, dimensions={2}, use_global_device_ids=true | all-gather | bytes 12800 | tf_op jit(solution)/shard_map/all_gather | solution.py:96
  21.1 11.8 %all_gather.24 = bf16[1,2,2560]{2,0,1:T(2,128)(2,1)S(1)} all-gather(bf16[1,2,640]{2,0,1:T(2,128)(2,1)S(1)} %copy.469), channel_id=1, replica_groups=mesh['seq'=64,'mp'=4] {'mp'}, dimensions={2}, use_global_device_ids=true | all-gather | bytes 12800 | tf_op jit(solution)/shard_map/all_gather | solution.py:96
  32.9 53.2 %all_gather.25 = bf16[1,128,2560]{2,0,1:T(2,128)(2,1)S(1)} all-gather(bf16[1,2,2560]{2,0,1:T(2,128)(2,1)S(1)} %all_gather.24), channel_id=1, replica_groups=mesh['seq'=64,'mp'=4] {'seq'}, dimensions={1}, use_global_device_ids=true | all-gather | bytes 665600 | tf_op jit(solution)/shard_map/all_gather | solution.py:97
  90.1 1.6 multiply_reduce_fusion.7
  91.7 48.7 %all_gather.29 = bf16[1,128,2560]{2,0,1:T(2,128)(2,1)S(1)} all-gather(bf16[1,2,2560]{2,0,1:T(2,128)(2,1)S(1)} %all_gather.28), channel_id=1, replica_groups=mesh['seq'=64,'mp'=4] {'seq'}, dimensions={1}, use_global_device_ids=true | all-gather | bytes 665600 | tf_op jit(solution)/shard_map/all_gather | solution.py:97
  141.7 1.6 multiply_reduce_fusion.5
  143.3 11.8 %all_gather.26 = bf16[1,2,2560]{2,0,1:T(2,128)(2,1)S(1)} all-gather(bf16[1,2,640]{2,0,1:T(2,128)(2,1)S(1)} %copy.472), channel_id=1, replica_groups=mesh['seq'=64,'mp'=4] {'mp'}, dimensions={2}, use_global_device_ids=true | all-gather | bytes 12800 | tf_op jit(solution)/shard_map/all_gather | solution.py:96
  155.1 49.3 %all_gather.27 = bf16[1,128,2560]{2,0,1:T(2,128)(2,1)S(1)} all-gather(bf16[1,2,2560]{2,0,1:T(2,128)(2,1)S(1)} %all_gather.26), channel_id=1, replica_groups=mesh['seq'=64,'mp'=4] {'seq'}, dimensions={1}, use_global_device_ids=true | all-gather | bytes 665600 | tf_op jit(solution)/shard_map/all_gather | solution.py:97
  205.7 1.7 multiply_reduce_fusion.6
  207.4 11.8 %all_gather.30 = bf16[1,2,2560]{2,0,1:T(2,128)(2,1)S(1)} all-gather(bf16[1,2,640]{2,0,1:T(2,128)(2,1)S(1)} %copy.478), channel_id=1, replica_groups=mesh['seq'=64,'mp'=4] {'mp'}, dimensions={2}, use_global_device_ids=true | all-gather | bytes 12800 | tf_op jit(solution)/shard_map/all_gather | solution.py:96
  219.3 48.6 %all_gather.31 = bf16[1,128,2560]{2,0,1:T(2,128)(2,1)S(1)} all-gather(bf16[1,2,2560]{2,0,1:T(2,128)(2,1)S(1)} %all_gather.30), channel_id=1, replica_groups=mesh['seq'=64,'mp'=4] {'seq'}, dimensions={1}, use_global_device_ids=true | all-gather | bytes 665600 | tf_op jit(solution)/shard_map/all_gather | solution.py:97
  269.2 1.6 multiply_reduce_fusion.4
  270.8 4.4 copy.463
  275.3 3.8 multiply_reduce_fusion.3
  279.1 2.2 multiply_reduce_fusion
  281.3 2.2 multiply_reduce_fusion.1
  283.7 1.6 multiply_reduce_fusion.2
  295.6 2.0 multiply_multiply_fusion.3
  306.6 1.7 fusion.29
  308.3 1.6 fusion.30
  312.0 109.9 %all-reduce.2 = (f32[1,128,1,4]{1,3,2,0:T(4,128)}, f32[1,128,1,4]{1,3,2,0:T(4,128)}, f32[1,128,1,4]{1,3,2,0:T(4,128)}, f32[1,128,1,4]{1,3,2,0:T(4,128)}) all-reduce(f32[1,128,1,4]{1,3,2,0:T(4,128)} %bitcast.554, f32[1,128,1,4]{1,3,2,0:T(4,128)S(1)} %bitcast.553, ...), channel_id=1, replica_groups=mesh['seq'=64,'mp'=4] {'seq'}, use_global_device_ids=true, to_apply=%region_39.42 | all-reduce | flops 2048 | bytes 16384 | tf_op jit(solution)/shard_map/pmax | solution.py:148
  431.2 1.6 fusion.111
  445.7 111.5 %all-reduce = (f32[1,128,1,4]{1,3,2,0:T(4,128)S(1)}, f32[1,128,1,4]{1,3,2,0:T(4,128)S(1)}, f32[1,128,1,4]{1,3,2,0:T(4,128)S(1)}, f32[1,128,1,4]{1,3,2,0:T(4,128)S(1)}) all-reduce(f32[1,128,1,4]{1,3,2,0:T(4,128)S(1)} %fusion.33, f32[1,128,1,4]{1,3,2,0:T(4,128)S(1)} %fusion.34, ...), channel_id=1, replica_groups=mesh['seq'=64,'mp'=4] {'seq'}, use_global_device_ids=true, to_apply=%region_43.46 | all-reduce | flops 2048 | bytes 16384 | tf_op jit(solution)/shard_map/psum | solution.py:150
  559.7 80.1 %all-reduce.5.cloned.1.call-done = (f32[1,128,1,4,128]{1,4,3,2,0:T(8,128)}, f32[1,128,1,4,128]{1,4,3,2,0:T(8,128)}, f32[1,128,1,4,128]{1,4,3,2,0:T(8,128)}, f32[1,128,1,4,128]{1,4,3,2,0:T(8,128)}) async-done(((f32[1,128,1,4,128]{1,4,3,2,0:T(8,128)}, f32[1,128,1,4,128]{1,4,3,2,0:T(8,128)}, f32[1,128,1,4,128]{1,4,3,2,0:T(8,128)}, f32[1,128,1,4,128]{1,4,3,2,0:T(8,128)}), (f32[1,128,1,4,128]{1,4,3,2,0:T(8,128)}, ...) | async-done | bytes 1048592 | tf_op jit(solution)/shard_map/psum | solution.py:150
  640.9 2.2 convolution_bitcast_fusion
  644.2 2.2 convolution_bitcast_fusion.1
  647.5 2.2 convolution_bitcast_fusion.2
  650.8 2.2 convolution_bitcast_fusion.3
  654.2 13.9 %reduce-scatter.19.cloned.1.call-done = f32[640,2]{1,0:T(8,128)} async-done(((f32[2560,2]{1,0:T(8,128)}), f32[640,2]{1,0:T(8,128)}) %reduce-scatter.19.cloned.1.call-update) | async-done | bytes 5136
  669.2 28.5 %reduce-scatter.17.cloned.1.call-done = f32[640,2]{1,0:T(8,128)} async-done(((f32[2560,2]{1,0:T(8,128)}), f32[640,2]{1,0:T(8,128)}) %reduce-scatter.17.cloned.1.call-update) | async-done | bytes 5136
  698.8 28.3 %reduce-scatter.15.cloned.1.call-done = f32[640,2]{1,0:T(8,128)} async-done(((f32[2560,2]{1,0:T(8,128)}), f32[640,2]{1,0:T(8,128)}) %reduce-scatter.15.cloned.1.call-update) | async-done | bytes 5136
  728.2 28.3 %reduce-scatter.13.cloned.1.call-done = f32[640,2]{1,0:T(8,128)} async-done(((f32[2560,2]{1,0:T(8,128)}), f32[640,2]{1,0:T(8,128)}) %reduce-scatter.13.cloned.1.call-update) | async-done | bytes 5136
  (365 shorter events, 65.3 us)
Async XLA Ops:
  7.2 633.7 %copy-start = (bf16[512,2560]{1,0:T(8,128)(2,1)S(1)}, bf16[512,2560]{1,0:T(8,128)(2,1)}, u32[]{:S(2)}) copy-start(bf16[512,2560]{1,0:T(8,128)(2,1)} %param.25) | copy-start | bytes 7864324
  7.2 632.6 %all-reduce.5.cloned.1.call-start = ((), (), s32[]{:S(2)}) async-start(), calls=%async_computation.8 | async-start | bytes 2097152 | tf_op jit(solution)/shard_map/psum | solution.py:150
  8.7 24.2 %copy-start.34 = (bf16[1,2,640]{2,1,0:T(2,128)(2,1)}, bf16[1,2,640]{2,1,0:T(2,128)(2,1)S(1)}, u32[]{:S(2)}) copy-start(bf16[1,2,640]{2,1,0:T(2,128)(2,1)S(1)} %get-tuple-element.84) | copy-start | bytes 7684
  8.7 24.2 %copy-start.38 = (bf16[1,2,640]{2,1,0:T(2,128)(2,1)}, bf16[1,2,640]{2,1,0:T(2,128)(2,1)S(1)}, u32[]{:S(2)}) copy-start(bf16[1,2,640]{2,1,0:T(2,128)(2,1)S(1)} %get-tuple-element.85) | copy-start | bytes 7684
  8.7 134.6 %copy-start.36 = (bf16[1,2,640]{2,1,0:T(2,128)(2,1)}, bf16[1,2,640]{2,1,0:T(2,128)(2,1)S(1)}, u32[]{:S(2)}) copy-start(bf16[1,2,640]{2,1,0:T(2,128)(2,1)S(1)} %get-tuple-element.86) | copy-start | bytes 7684
  8.7 198.7 %copy-start.40 = (bf16[1,2,640]{2,1,0:T(2,128)(2,1)}, bf16[1,2,640]{2,1,0:T(2,128)(2,1)S(1)}, u32[]{:S(2)}) copy-start(bf16[1,2,640]{2,1,0:T(2,128)(2,1)S(1)} %get-tuple-element.87) | copy-start | bytes 7684
  283.6 7.1 copy-start.69
  283.6 7.1 copy-start.12
  283.6 7.1 copy-start.22
  283.6 7.1 copy-start.23
  283.6 7.1 copy-start.24
  283.6 7.1 copy-start.62
  285.3 10.3 %copy-start.60 = (f32[128,4]{0,1:T(4,128)S(1)}, f32[128,4]{0,1:T(4,128)}, u32[]{:S(2)}) copy-start(f32[128,4]{0,1:T(4,128)} %get-tuple-element.150) | copy-start | bytes 6148
  285.3 10.3 %copy-start.59 = (f32[128,4]{0,1:T(4,128)S(1)}, f32[128,4]{0,1:T(4,128)}, u32[]{:S(2)}) copy-start(f32[128,4]{0,1:T(4,128)} %get-tuple-element.152) | copy-start | bytes 6148
  285.3 10.3 %copy-start.55 = (f32[128,4]{0,1:T(4,128)S(1)}, f32[128,4]{0,1:T(4,128)}, u32[]{:S(2)}) copy-start(f32[128,4]{0,1:T(4,128)} %get-tuple-element.146) | copy-start | bytes 6148
  285.3 25.0 %copy-start.45 = (pred[16]{0:T(512)(128)(4,1)}, pred[16]{0:T(512)(128)(4,1)S(1)}, u32[]{:S(2)}) copy-start(pred[16]{0:T(512)(128)(4,1)S(1)} %broadcast_compare_fusion) | copy-start | bytes 52
  286.5 19.3 %copy-start.42 = (s32[1024]{0:T(1024)}, s32[1024]{0:T(1024)S(1)}, u32[]{:S(2)}) copy-start(s32[1024]{0:T(1024)S(1)} %pad_clamp_fusion) | copy-start | bytes 12292
  287.7 18.7 %copy-start.58 = (pred[16]{0:T(512)(128)(4,1)}, pred[16]{0:T(512)(128)(4,1)S(1)}, u32[]{:S(2)}) copy-start(pred[16]{0:T(512)(128)(4,1)S(1)} %get-tuple-element.53) | copy-start | bytes 52
  311.4 114.5 %copy-start.25 = (f32[128,4]{0,1:T(4,128)}, f32[128,4]{0,1:T(4,128)S(1)}, u32[]{:S(2)}) copy-start(f32[128,4]{0,1:T(4,128)S(1)} %get-tuple-element.28) | copy-start | bytes 6148
  311.4 114.5 %copy-start.27 = (f32[128,4]{0,1:T(4,128)}, f32[128,4]{0,1:T(4,128)S(1)}, u32[]{:S(2)}) copy-start(f32[128,4]{0,1:T(4,128)S(1)} %get-tuple-element.31) | copy-start | bytes 6148
  436.2 6.8 copy-start.49
  437.3 6.7 copy-start.47
  437.3 7.2 copy-start.50
  438.5 6.8 copy-start.26
  439.6 228.5 %reduce-scatter.19.cloned.1.call-start = ((), (), s32[]{:S(2)}) async-start(), calls=%async_computation.7 | async-start | bytes 1638400
  643.1 54.5 %reduce-scatter.17.cloned.1.call-start = ((), (), s32[]{:S(2)}) async-start(), calls=%async_computation.6 | async-start | bytes 1638400
  646.4 80.6 %reduce-scatter.15.cloned.1.call-start = ((), (), s32[]{:S(2)}) async-start(), calls=%async_computation.5 | async-start | bytes 1638400
  649.7 106.7 %reduce-scatter.13.cloned.1.call-start = ((), (), s32[]{:S(2)}) async-start(), calls=%async_computation.4 | async-start | bytes 1638400
  653.0 104.5 %copy-start.39 = (bf16[1,2,640]{2,1,0:T(2,128)(2,1)S(1)}, bf16[1,2,640]{2,1,0:T(2,128)(2,1)}, u32[]{:S(2)}) copy-start(bf16[1,2,640]{2,1,0:T(2,128)(2,1)} %copy-done.38) | copy-start | bytes 7684
  653.0 104.5 %copy-start.41 = (bf16[1,2,640]{2,1,0:T(2,128)(2,1)S(1)}, bf16[1,2,640]{2,1,0:T(2,128)(2,1)}, u32[]{:S(2)}) copy-start(bf16[1,2,640]{2,1,0:T(2,128)(2,1)} %copy-done.40) | copy-start | bytes 7684
  653.0 104.6 %copy-start.35 = (bf16[1,2,640]{2,1,0:T(2,128)(2,1)S(1)}, bf16[1,2,640]{2,1,0:T(2,128)(2,1)}, u32[]{:S(2)}) copy-start(bf16[1,2,640]{2,1,0:T(2,128)(2,1)} %copy-done.34) | copy-start | bytes 7684
  653.0 104.6 %copy-start.37 = (bf16[1,2,640]{2,1,0:T(2,128)(2,1)S(1)}, bf16[1,2,640]{2,1,0:T(2,128)(2,1)}, u32[]{:S(2)}) copy-start(bf16[1,2,640]{2,1,0:T(2,128)(2,1)} %copy-done.36) | copy-start | bytes 7684
  (49 other events, 153.2 us)
Sparse Core Ops, SparseCore 0:
  439.8 199.9 all-reduce.4
  643.3 24.8 reduce-scatter.18
  670.8 26.7 reduce-scatter.16
  700.2 26.7 reduce-scatter.14
  729.6 26.7 reduce-scatter.12
where the time goes:
time: 766 us; the launch traced here: 765 us
  blocking collectives  469 us (61%)
  waiting for transfers between devices  179 us (23%)
  matrix products  43.9 us (6%)
  local copies, waits for them, and re-layouts  32.9 us (4%)
  other arithmetic  24.7 us (3%)
  between operations  14.9 us (2%)
    all_gather x4, blocking collectives, shards(): portion = lax.all_gather(wide_states, 'seq', axis=1, tiled=True)  200 us
    psum x1, blocking collectives, shards(): lax.psum((row_total * every_factor, row_mix * every_factor[..., None]), '...  112 us
    pmax x1, blocking collectives, shards(): every_top = lax.pmax(row_top, 'seq')  110 us
    unnamed x9, waiting for transfers between devices  99 us
    psum x1, waiting for transfers between devices, shards(): lax.psum((row_total * every_factor, row_mix * every_factor[..., None]), '...  80.1 us
    all_gather x4, blocking collectives, shards(): wide_states = lax.all_gather(block_states, 'mp', axis=2, tiled=True)  47.8 us
  transfers between devices with their start and end apart: 5, of which 5 were waited for; matrix products, arithmetic and copies ran while one was open for 3% of the time, Pallas kernels for 0%

commit v1 on v0

--- a/solution.py
+++ b/solution.py
@@ -93,7 +93,14 @@
         number = high_turn - low_turn
         turn_ids = jnp.arange(low_turn, high_turn, dtype=jnp.int32)
         block_states = states[low_turn:high_turn]
-        wide_states = lax.all_gather(block_states, "mp", axis=2, tiled=True)
+        ring = [block_states]
+        for hop in range(3):
+            ring.append(lax.ppermute(ring[-1], "mp", [(dev, (dev + 1) % 4) for dev in range(4)]))
+        wide_states = jnp.roll(
+            jnp.concatenate(ring[::-1], axis=2),
+            (lax.axis_index("mp") + 1) * ring[0].shape[2],
+            axis=2,
+        )
         portion = lax.all_gather(wide_states, "seq", axis=1, tiled=True)
         portion_rows = portion.shape[1]
         portion_positions = req_len[None, :] + turn_ids[:, None]

time: 766 us -> 882 us (1.15)
  waiting for transfers between devices: 179 us -> 311 us
  blocking collectives: 469 us -> 422 us
  starting transfers between devices: 0.21 us -> 14.3 us
  other arithmetic: 24.7 us -> 34 us
  local copies, waits for them, and re-layouts: 32.9 us -> 42.1 us
  matrix products: 43.9 us -> 35 us
    psum x1, waiting for transfers between devices: 80.1 us -> 212 us  [shards(): lax.psum((row_total * every_factor, row_mix * every_factor[..., None]), '...]
    all_gather x4 -> x0, blocking collectives: 47.8 us -> none  [shards(): wide_states = lax.all_gather(block_states, 'mp', axis=2, tiled=True)]
    ppermute x0 -> x12, starting transfers between devices: none -> 14.1 us  [shards(): lax.ppermute(ring[-1], 'mp', [(dev, (dev + 1) % 4) for dev in range(4)])]
  transfers between devices with their start and end apart: 5 -> 17, of which waited for: 5 -> 5; matrix products, arithmetic and copies ran while one was open for 3% -> 4% of each run, Pallas kernels for 0% -> 0%
where the time goes in v1:
time: 882 us; the launch traced here: 873 us
  blocking collectives  422 us (48%)
  waiting for transfers between devices  311 us (35%)
  local copies, waits for them, and re-layouts  42.1 us (5%)
  matrix products  35 us (4%)
  other arithmetic  34 us (4%)
  between operations  14.9 us (2%)
  starting transfers between devices  14.3 us (2%)
    psum x1, waiting for transfers between devices, shards(): lax.psum((row_total * every_factor, row_mix * every_factor[..., None]), '...  212 us
    all_gather x4, blocking collectives, shards(): portion = lax.all_gather(wide_states, 'seq', axis=1, tiled=True)  200 us
    psum x1, blocking collectives, shards(): lax.psum((row_total * every_factor, row_mix * every_factor[..., None]), '...  112 us
    pmax x1, blocking collectives, shards(): every_top = lax.pmax(row_top, 'seq')  109 us
    unnamed x9, waiting for transfers between devices  98.4 us
  transfers between devices with their start and end apart: 17, of which 5 were waited for; matrix products, arithmetic and copies ran while one was open for 4% of the time, Pallas kernels for 0%

profile of v1, /device:TPU:2, one launch (start us, length us, event | category | flops | bytes accessed | tf_op | source)
XLA Modules:
  0.0 872.8 jit_solution(7436740208250572820)
XLA Ops:
  8.7 1.6 collective-permute-start.9
  10.3 1.6 collective-permute-start.3
  21.8 1.6 collective-permute-start.1
  23.9 1.6 collective-permute-start.10
  27.0 1.6 collective-permute-start.2
  29.2 4.4 copy.463
  33.6 1.7 collective-permute-start.11
  37.1 53.7 %all_gather.12 = bf16[1,128,2560]{2,0,1:T(2,128)(2,1)S(1)} all-gather(bf16[1,2,2560]{2,0,1:T(2,128)(2,1)S(1)} %fusion.159), channel_id=1, replica_groups=mesh['seq'=64,'mp'=4] {'seq'}, dimensions={1}, use_global_device_ids=true | all-gather | bytes 665600 | tf_op jit(solution)/shard_map/all_gather | solution.py:104
  95.0 48.7 %all_gather.14 = bf16[1,128,2560]{2,0,1:T(2,128)(2,1)S(1)} all-gather(bf16[1,2,2560]{2,0,1:T(2,128)(2,1)S(1)} %fusion.161), channel_id=1, replica_groups=mesh['seq'=64,'mp'=4] {'seq'}, dimensions={1}, use_global_device_ids=true | all-gather | bytes 665600 | tf_op jit(solution)/shard_map/all_gather | solution.py:104
  145.9 49.2 %all_gather.13 = bf16[1,128,2560]{2,0,1:T(2,128)(2,1)S(1)} all-gather(bf16[1,2,2560]{2,0,1:T(2,128)(2,1)S(1)} %fusion.160), channel_id=1, replica_groups=mesh['seq'=64,'mp'=4] {'seq'}, dimensions={1}, use_global_device_ids=true | all-gather | bytes 665600 | tf_op jit(solution)/shard_map/all_gather | solution.py:104
  197.2 48.9 %all_gather.15 = bf16[1,128,2560]{2,0,1:T(2,128)(2,1)S(1)} all-gather(bf16[1,2,2560]{2,0,1:T(2,128)(2,1)S(1)} %fusion.162), channel_id=1, replica_groups=mesh['seq'=64,'mp'=4] {'seq'}, dimensions={1}, use_global_device_ids=true | all-gather | bytes 665600 | tf_op jit(solution)/shard_map/all_gather | solution.py:104
  248.9 1.6 multiply_reduce_fusion
  250.6 1.6 multiply_reduce_fusion.1
  252.2 1.6 multiply_reduce_fusion.2
  257.1 2.0 multiply_multiply_fusion.3
  259.9 1.7 fusion.248
  268.0 1.5 fusion.249
  285.1 1.7 fusion.29
  286.8 1.6 fusion.30
  293.1 1.6 fusion.111
  294.7 1.5 fusion.114
  298.7 109.0 %all-reduce.2 = (f32[1,128,1,4]{1,3,2,0:T(4,128)S(1)}, f32[1,128,1,4]{1,3,2,0:T(4,128)S(1)}, f32[1,128,1,4]{1,3,2,0:T(4,128)S(1)}, f32[1,128,1,4]{1,3,2,0:T(4,128)S(1)}) all-reduce(f32[1,128,1,4]{1,3,2,0:T(4,128)S(1)} %bitcast.554, f32[1,128,1,4]{1,3,2,0:T(4,128)S(1)} %bitcast.553, ...), channel_id=1, replica_groups=mesh['seq'=64,'mp'=4] {'seq'}, use_global_device_ids=true, to_apply=%region_39.43 | all-reduce | flops 2048 | bytes 16384 | tf_op jit(solution)/shard_map/pmax | solution.py:155
  414.2 112.3 %all-reduce = (f32[1,128,1,4]{1,3,2,0:T(4,128)}, f32[1,128,1,4]{1,3,2,0:T(4,128)}, f32[1,128,1,4]{1,3,2,0:T(4,128)S(1)}, f32[1,128,1,4]{1,3,2,0:T(4,128)S(1)}) all-reduce(f32[1,128,1,4]{1,3,2,0:T(4,128)S(1)} %fusion.33, f32[1,128,1,4]{1,3,2,0:T(4,128)S(1)} %fusion.34, ...), channel_id=1, replica_groups=mesh['seq'=64,'mp'=4] {'seq'}, use_global_device_ids=true, to_apply=%region_43.47 | all-reduce | flops 2048 | bytes 16384 | tf_op jit(solution)/shard_map/psum | solution.py:157
  535.3 212.3 %all-reduce.5.cloned.1.call-done = (f32[1,128,1,4,128]{1,4,3,2,0:T(8,128)}, f32[1,128,1,4,128]{1,4,3,2,0:T(8,128)}, f32[1,128,1,4,128]{1,4,3,2,0:T(8,128)}, f32[1,128,1,4,128]{1,4,3,2,0:T(8,128)}) async-done(((f32[1,128,1,4,128]{1,4,3,2,0:T(8,128)}, f32[1,128,1,4,128]{1,4,3,2,0:T(8,128)}, f32[1,128,1,4,128]{1,4,3,2,0:T(8,128)}, f32[1,128,1,4,128]{1,4,3,2,0:T(8,128)}), (f32[1,128,1,4,128]{1,4,3,2,0:T(8,128)}, ...) | async-done | bytes 1048592 | tf_op jit(solution)/shard_map/psum | solution.py:157
  748.7 2.2 convolution_bitcast_fusion
  752.0 2.2 convolution_bitcast_fusion.1
  755.3 2.2 convolution_bitcast_fusion.2
  758.6 2.2 convolution_bitcast_fusion.3
  762.7 13.2 %reduce-scatter.19.cloned.1.call-done = f32[640,2]{1,0:T(8,128)} async-done(((f32[2560,2]{1,0:T(8,128)}), f32[640,2]{1,0:T(8,128)}) %reduce-scatter.19.cloned.1.call-update) | async-done | bytes 5136
  777.0 28.5 %reduce-scatter.17.cloned.1.call-done = f32[640,2]{1,0:T(8,128)} async-done(((f32[2560,2]{1,0:T(8,128)}), f32[640,2]{1,0:T(8,128)}) %reduce-scatter.17.cloned.1.call-update) | async-done | bytes 5136
  806.6 28.3 %reduce-scatter.15.cloned.1.call-done = f32[640,2]{1,0:T(8,128)} async-done(((f32[2560,2]{1,0:T(8,128)}), f32[640,2]{1,0:T(8,128)}) %reduce-scatter.15.cloned.1.call-update) | async-done | bytes 5136
  836.0 28.3 %reduce-scatter.13.cloned.1.call-done = f32[640,2]{1,0:T(8,128)} async-done(((f32[2560,2]{1,0:T(8,128)}), f32[640,2]{1,0:T(8,128)}) %reduce-scatter.13.cloned.1.call-update) | async-done | bytes 5136
  (356 shorter events, 86.3 us)
Async XLA Ops:
  7.2 741.5 %copy-start = (bf16[512,2560]{1,0:T(8,128)(2,1)S(1)}, bf16[512,2560]{1,0:T(8,128)(2,1)}, u32[]{:S(2)}) copy-start(bf16[512,2560]{1,0:T(8,128)(2,1)} %param.27) | copy-start | bytes 7864324
  7.2 740.4 %all-reduce.5.cloned.1.call-start = ((), (), s32[]{:S(2)}) async-start(), calls=%async_computation.8 | async-start | bytes 2097152 | tf_op jit(solution)/shard_map/psum | solution.py:157
  8.7 15.2 %collective-permute-start.9 = (bf16[1,2,640]{2,0,1:T(2,128)(2,1)S(1)}, bf16[1,2,640]{2,0,1:T(2,128)(2,1)S(1)}, u32[]{:S(2)}, u32[]{:S(2)}) collective-permute-start(bf16[1,2,640]{2,0,1:T(2,128)(2,1)S(1)} %copy.478), channel_id=1, source_target_pairs={{0,1},{1,2},{2,3},{3,0},{4,5},{5,6},{6,7},{7,4},{8,9},{9,10},{10,1... | collective-permute-start | bytes 7688 | tf_op jit(solution)/shard_map/ppermute | solution.py:98
  10.3 15.2 %collective-permute-start.3 = (bf16[1,2,640]{2,0,1:T(2,128)(2,1)S(1)}, bf16[1,2,640]{2,0,1:T(2,128)(2,1)S(1)}, u32[]{:S(2)}, u32[]{:S(2)}) collective-permute-start(bf16[1,2,640]{2,0,1:T(2,128)(2,1)S(1)} %copy.472), channel_id=1, source_target_pairs={{0,1},{1,2},{2,3},{3,0},{4,5},{5,6},{6,7},{7,4},{8,9},{9,10},{10,1... | collective-permute-start | bytes 7688 | tf_op jit(solution)/shard_map/ppermute | solution.py:98
  11.9 14.9 %collective-permute-start.6 = (bf16[1,2,640]{2,0,1:T(2,128)(2,1)S(1)}, bf16[1,2,640]{2,0,1:T(2,128)(2,1)S(1)}, u32[]{:S(2)}, u32[]{:S(2)}) collective-permute-start(bf16[1,2,640]{2,0,1:T(2,128)(2,1)S(1)} %copy.475), channel_id=1, source_target_pairs={{0,1},{1,2},{2,3},{3,0},{4,5},{5,6},{6,7},{7,4},{8,9},{9,10},{10,1... | collective-permute-start | bytes 7688 | tf_op jit(solution)/shard_map/ppermute | solution.py:98
  13.2 8.6 collective-permute-start
  13.4 241.8 %copy-start.43 = (f32[64]{0:T(128)}, f32[64]{0:T(128)S(1)}, u32[]{:S(2)}) copy-start(f32[64]{0:T(128)S(1)} %multiply_power_fusion) | copy-start | bytes 772
  14.1 19.5 %copy-start.23 = (pred[16]{0:T(512)(128)(4,1)}, pred[16]{0:T(512)(128)(4,1)S(1)}, u32[]{:S(2)}) copy-start(pred[16]{0:T(512)(128)(4,1)S(1)} %broadcast_compare_fusion) | copy-start | bytes 52
  17.4 16.1 %copy-start.44 = (f32[128]{0:T(128)}, f32[128]{0:T(128)S(1)}, u32[]{:S(2)}) copy-start(f32[128]{0:T(128)S(1)} %get-tuple-element.132) | copy-start | bytes 1540
  21.8 5.2 collective-permute-start.1
  23.9 9.7 %collective-permute-start.10 = (bf16[1,2,640]{2,0,1:T(2,128)(2,1)S(1)}, bf16[1,2,640]{2,0,1:T(2,128)(2,1)S(1)}, u32[]{:S(2)}, u32[]{:S(2)}) collective-permute-start(bf16[1,2,640]{2,0,1:T(2,128)(2,1)S(1)} %collective-permute-done.9), channel_id=1, source_target_pairs={{0,1},{1,2},{2,3},{3,0},{4,5},{5,6},{6,7},{7,4},{8,9},{9,10},{10,1... | collective-permute-start | bytes 7688 | tf_op jit(solution)/shard_map/ppermute | solution.py:98
  25.5 9.7 %collective-permute-start.4 = (bf16[1,2,640]{2,0,1:T(2,128)(2,1)S(1)}, bf16[1,2,640]{2,0,1:T(2,128)(2,1)S(1)}, u32[]{:S(2)}, u32[]{:S(2)}) collective-permute-start(bf16[1,2,640]{2,0,1:T(2,128)(2,1)S(1)} %collective-permute-done.3), channel_id=1, source_target_pairs={{0,1},{1,2},{2,3},{3,0},{4,5},{5,6},{6,7},{7,4},{8,9},{9,10},{10,1... | collective-permute-start | bytes 7688 | tf_op jit(solution)/shard_map/ppermute | solution.py:98
  26.8 9.7 %collective-permute-start.7 = (bf16[1,2,640]{2,0,1:T(2,128)(2,1)S(1)}, bf16[1,2,640]{2,0,1:T(2,128)(2,1)S(1)}, u32[]{:S(2)}, u32[]{:S(2)}) collective-permute-start(bf16[1,2,640]{2,0,1:T(2,128)(2,1)S(1)} %collective-permute-done.6), channel_id=1, source_target_pairs={{0,1},{1,2},{2,3},{3,0},{4,5},{5,6},{6,7},{7,4},{8,9},{9,10},{10,1... | collective-permute-start | bytes 7688 | tf_op jit(solution)/shard_map/ppermute | solution.py:98
  27.0 9.7 %collective-permute-start.2 = (bf16[1,2,640]{2,0,1:T(2,128)(2,1)S(1)}, bf16[1,2,640]{2,0,1:T(2,128)(2,1)S(1)}, u32[]{:S(2)}, u32[]{:S(2)}) collective-permute-start(bf16[1,2,640]{2,0,1:T(2,128)(2,1)S(1)} %collective-permute-done.1), channel_id=1, source_target_pairs={{0,1},{1,2},{2,3},{3,0},{4,5},{5,6},{6,7},{7,4},{8,9},{9,10},{10,1... | collective-permute-start | bytes 7688 | tf_op jit(solution)/shard_map/ppermute | solution.py:98
  33.6 163.3 %collective-permute-start.11 = (bf16[1,2,640]{2,0,1:T(2,128)(2,1)S(1)}, bf16[1,2,640]{2,0,1:T(2,128)(2,1)S(1)}, u32[]{:S(2)}, u32[]{:S(2)}) collective-permute-start(bf16[1,2,640]{2,0,1:T(2,128)(2,1)S(1)} %collective-permute-done.10), channel_id=1, source_target_pairs={{0,1},{1,2},{2,3},{3,0},{4,5},{5,6},{6,7},{7,4},{8,9},{9,10},{10,1... | collective-permute-start | bytes 7688 | tf_op jit(solution)/shard_map/ppermute | solution.py:98
  35.2 110.3 %collective-permute-start.5 = (bf16[1,2,640]{2,0,1:T(2,128)(2,1)S(1)}, bf16[1,2,640]{2,0,1:T(2,128)(2,1)S(1)}, u32[]{:S(2)}, u32[]{:S(2)}) collective-permute-start(bf16[1,2,640]{2,0,1:T(2,128)(2,1)S(1)} %collective-permute-done.4), channel_id=1, source_target_pairs={{0,1},{1,2},{2,3},{3,0},{4,5},{5,6},{6,7},{7,4},{8,9},{9,10},{10,1... | collective-permute-start | bytes 7688 | tf_op jit(solution)/shard_map/ppermute | solution.py:98
  36.5 58.2 %collective-permute-start.8 = (bf16[1,2,640]{2,0,1:T(2,128)(2,1)S(1)}, bf16[1,2,640]{2,0,1:T(2,128)(2,1)S(1)}, u32[]{:S(2)}, u32[]{:S(2)}) collective-permute-start(bf16[1,2,640]{2,0,1:T(2,128)(2,1)S(1)} %collective-permute-done.7), channel_id=1, source_target_pairs={{0,1},{1,2},{2,3},{3,0},{4,5},{5,6},{6,7},{7,4},{8,9},{9,10},{10,1... | collective-permute-start | bytes 7688 | tf_op jit(solution)/shard_map/ppermute | solution.py:98
  259.9 12.2 %copy-start.9 = (f32[128,1,128]{0,2,1:T(8,128)S(1)}, f32[128,1,128]{0,2,1:T(8,128)}, u32[]{:S(2)}) copy-start(f32[128,1,128]{0,2,1:T(8,128)} %get-tuple-element.136) | copy-start | bytes 196612
  259.9 13.8 %copy-start.15 = (f32[128,64]{0,1:T(8,128)S(1)}, f32[128,64]{0,1:T(8,128)}, u32[]{:S(2)}) copy-start(f32[128,64]{0,1:T(8,128)} %get-tuple-element.117) | copy-start | bytes 98308
  259.9 13.8 %copy-start.16 = (f32[128,64]{0,1:T(8,128)S(1)}, f32[128,64]{0,1:T(8,128)}, u32[]{:S(2)}) copy-start(f32[128,64]{0,1:T(8,128)} %get-tuple-element.118) | copy-start | bytes 98308
  269.5 9.5 %copy-start.14 = (f32[128,64]{0,1:T(8,128)S(1)}, f32[128,64]{0,1:T(8,128)}, u32[]{:S(2)}) copy-start(f32[128,64]{0,1:T(8,128)} %get-tuple-element.99) | copy-start | bytes 98308
  296.7 116.6 %copy-start.22 = (s32[16]{0:T(128)S(1)}, s32[16]{0:T(128)}, u32[]{:S(2)}) copy-start(s32[16]{0:T(128)} %param.31) | copy-start | bytes 196
  296.7 116.6 %copy-start.24 = (pred[16]{0:T(512)(128)(4,1)S(1)}, pred[16]{0:T(512)(128)(4,1)}, u32[]{:S(2)}) copy-start(pred[16]{0:T(512)(128)(4,1)} %copy-done.23) | copy-start | bytes 52
  407.8 124.5 %copy-start.25 = (f32[1,128,1,4]{1,3,2,0:T(4,128)}, f32[1,128,1,4]{1,3,2,0:T(4,128)S(1)}, u32[]{:S(2)}) copy-start(f32[1,128,1,4]{1,3,2,0:T(4,128)S(1)} %get-tuple-element.41) | copy-start | bytes 6148
  408.5 123.8 %copy-start.26 = (f32[1,2,1,4]{1,3,2,0:T(4,128)}, f32[1,2,1,4]{1,3,2,0:T(4,128)S(1)}, u32[]{:S(2)}) copy-start(f32[1,2,1,4]{1,3,2,0:T(4,128)S(1)} %get-tuple-element.52) | copy-start | bytes 100
  412.0 120.3 %copy-start.27 = (f32[1,2,1,4]{1,3,2,0:T(4,128)}, f32[1,2,1,4]{1,3,2,0:T(4,128)S(1)}, u32[]{:S(2)}) copy-start(f32[1,2,1,4]{1,3,2,0:T(4,128)S(1)} %get-tuple-element.50) | copy-start | bytes 100
  531.1 216.5 %copy-start.31 = (f32[2,4]{0,1:T(4,128)S(1)}, f32[2,4]{0,1:T(4,128)}, u32[]{:S(2)}) copy-start(f32[2,4]{0,1:T(4,128)} %get-tuple-element.51) | copy-start | bytes 100
  532.3 243.7 %reduce-scatter.19.cloned.1.call-start = ((), (), s32[]{:S(2)}) async-start(), calls=%async_computation.7 | async-start | bytes 1638400
  750.9 54.5 %reduce-scatter.17.cloned.1.call-start = ((), (), s32[]{:S(2)}) async-start(), calls=%async_computation.6 | async-start | bytes 1638400
  754.2 80.6 %reduce-scatter.15.cloned.1.call-start = ((), (), s32[]{:S(2)}) async-start(), calls=%async_computation.5 | async-start | bytes 1638400
  757.6 106.7 %reduce-scatter.13.cloned.1.call-start = ((), (), s32[]{:S(2)}) async-start(), calls=%async_computation.4 | async-start | bytes 1638400
  760.8 104.5 %copy-start.19 = (bf16[1,2,640]{2,1,0:T(2,128)(2,1)S(1)}, bf16[1,2,640]{2,1,0:T(2,128)(2,1)}, u32[]{:S(2)}) copy-start(bf16[1,2,640]{2,1,0:T(2,128)(2,1)} %copy-done.18) | copy-start | bytes 7684
  (45 other events, 89.7 us)
Sparse Core Ops, SparseCore 0:
  532.4 215.1 all-reduce.4
  751.1 24.8 reduce-scatter.18
  778.7 26.7 reduce-scatter.16
  808.1 26.7 reduce-scatter.14
  837.5 26.7 reduce-scatter.12
